TPU v7x, 256 devices: a whole 4x4x8 slice. The times are simulated.
256 devices in a mesh: rows: 16 (over x, y), sub: 16 (over z, core).
Axes of the slice: x: 4, y: 4, z: 8, core: 2. Of those that a mesh axis runs over, the one named last changes fastest.
Arguments:
- embeddings: bfloat16 [65536, 1024], P(('rows', 'sub'))
- codes: int32 [64, 65536], P(None, ('rows', 'sub')), may hold values from 0 to 255
- codebook: bfloat16 [256, 1024], P(None, 'sub'), may hold values from -6 to 6
Outputs:
- rotation: float32 [1024, 1024], P('sub')
- rotated: bfloat16 [65536, 1024], P(('rows', 'sub'))
- new_codebook: float32 [256, 1024], P(None, 'sub')
All inputs are finite; a program needn't handle non-finite values.
Results may differ from a plain program's by a relative error of at most 0.0095.
Values may be sent and summed in bfloat16 or wider, within the bound.
No kernel may reach another device: no remote copies, remote signals or barrier semaphores. Data moves between devices by JAX's collectives and lax.ppermute only.
A program may use at most 64 MiB of HBM per device.

v0:
```python
import math
import jax
import jax.numpy as jnp
from jax import lax
from jax.sharding import PartitionSpec as P

NS_STEPS = 3
coef_a = 3.4445
coef_b = -4.775
coef_c = 2.0315
frob_eps = 1e-07
highest = lax.Precision.HIGHEST


def rows_dot(left, right):
    return lax.dot_general(
        left, right, (((1,), (1,)), ((), ())), precision=highest, preferred_element_type=jnp.float32
    )


def one_hot_codes(code_block, count_codes):
    levels = lax.broadcasted_iota(jnp.int32, code_block.shape + (count_codes,), 2)
    return (code_block[:, :, None] == levels).astype(jnp.bfloat16)


def decode_rows(codes, table):
    subspaces, local_rows = codes.shape
    count_codes, row_width = table.shape
    sub_width = row_width // subspaces
    block_rows = math.gcd(local_rows, 32768 // subspaces)
    blocks = local_rows // block_rows
    codewords = table.reshape(count_codes, subspaces, sub_width)
    code_blocks = codes.reshape(subspaces, blocks, block_rows).transpose(1, 0, 2)

    def decode_block(unused, code_block):
        one_hot = one_hot_codes(code_block, count_codes)
        picked = jnp.einsum("mnk,kmj->nmj", one_hot, codewords, preferred_element_type=jnp.float32)
        return (unused, picked.reshape(block_rows, row_width).astype(jnp.bfloat16))

    unused, decoded = lax.scan(decode_block, jnp.zeros((), jnp.float32), code_blocks)
    return decoded.reshape(local_rows, row_width)


def codeword_totals(codes, row_values, count_codes):
    subspaces, total_rows = codes.shape
    row_width = row_values.shape[1]
    sub_width = row_width // subspaces
    block_rows = math.gcd(total_rows, 32768 // subspaces)
    blocks = total_rows // block_rows
    code_blocks = codes.reshape(subspaces, blocks, block_rows).transpose(1, 0, 2)
    row_blocks = row_values.reshape(blocks, block_rows, subspaces, sub_width)

    def accumulate(running, pieces):
        one_hot = one_hot_codes(pieces[0], count_codes)
        block_sums = jnp.einsum(
            "mnk,nmj->kmj", one_hot, pieces[1], preferred_element_type=jnp.float32
        )
        block_counts = jnp.sum(one_hot, axis=1, dtype=jnp.float32).T
        return ((running[0] + block_sums, running[1] + block_counts), None)

    initial = (
        jnp.zeros((count_codes, subspaces, sub_width), jnp.float32),
        jnp.zeros((count_codes, subspaces), jnp.float32),
    )
    (code_sums, counts), unused = lax.scan(accumulate, initial, (code_blocks, row_blocks))
    return (code_sums.reshape(count_codes, row_width), counts)


def newton_panel(panel, whole):
    gram_rows = rows_dot(panel, whole)
    quartic = rows_dot(
        jnp.dot(gram_rows, whole, precision=highest, preferred_element_type=jnp.float32), whole
    )
    mixer = coef_b * gram_rows + coef_c * quartic
    return coef_a * panel + jnp.dot(
        mixer, whole, precision=highest, preferred_element_type=jnp.float32
    )


def collect(panel):
    return lax.all_gather(panel, "sub", axis=0, tiled=True)


def body(embeddings, codes, codebook):
    table = lax.all_gather(codebook, "sub", axis=1, tiled=True)
    decoded = decode_rows(codes, table)
    partial_panel = lax.psum_scatter(
        lax.dot_general(
            embeddings, decoded, (((0,), (0,)), ((), ())), preferred_element_type=jnp.float32
        ),
        "sub",
        scatter_dimension=0,
        tiled=True,
    )
    cross_panel = lax.psum(partial_panel, "rows")
    squares = lax.psum(jnp.sum(cross_panel * cross_panel), "sub")
    frob_scale = jnp.sqrt(squares) + frob_eps
    panel = cross_panel / frob_scale
    whole = collect(panel)
    for newton_step in range(NS_STEPS):
        if newton_step > 0:
            whole = collect(panel)
        panel = newton_panel(panel, whole)
    rotation_full = lax.all_gather(panel.astype(jnp.bfloat16), "sub", axis=0, tiled=True)
    rotated = jnp.dot(embeddings, rotation_full, preferred_element_type=jnp.float32).astype(
        jnp.bfloat16
    )
    moved_rows = lax.all_to_all(rotated, "sub", split_axis=1, concat_axis=0, tiled=True)
    moved_codes = lax.all_to_all(codes, "sub", split_axis=0, concat_axis=1, tiled=True)
    code_sums, counts = codeword_totals(moved_codes, moved_rows, table.shape[0])
    code_sums, counts = (
        lax.psum(code_sums.astype(jnp.bfloat16), "rows").astype(jnp.float32),
        lax.psum(counts.astype(jnp.bfloat16), "rows").astype(jnp.float32),
    )
    own_codebook = codebook.astype(jnp.float32)
    spread = jnp.repeat(counts, own_codebook.shape[1] // counts.shape[1], axis=1)
    new_codebook = (code_sums + own_codebook) / (spread + 1.0)
    return (panel, rotated, new_codebook)


def solution(mesh):
    in_specs = (P(("rows", "sub"), None), P(None, ("rows", "sub")), P(None, "sub"))
    out_specs = (P("sub", None), P(("rows", "sub"), None), P(None, "sub"))
    return jax.shard_map(body, mesh=mesh, in_specs=in_specs, out_specs=out_specs, check_vma=False)
```

profile of v0, /device:TPU:64, one launch (start us, length us, event | category | flops | bytes accessed | tf_op | source)
XLA Modules:
  0.0 547.7 jit_solution(3402713358330620616)
XLA Ops:
  7.2 0.0 copy-start
  7.2 0.0 reduce-scatter.4.cloned.1.call-start
  7.2 18.8 %all_gather.15 = bf16[256,1024]{0,1:T(8,128)(2,1)S(1)} all-gather(bf16[256,64]{0,1:T(8,128)(2,1)} %param.5), channel_id=1, replica_groups=mesh['rows'=16,'sub'=16] {'sub'}, dimensions={1}, use_global_device_ids=true | all-gather | bytes 557056 | tf_op jit(solution)/shard_map/all_gather | solution.py:85
  26.0 5.3 fusion.6
  31.3 0.0 copy-done
  31.3 2.7 convolution_bitcast_fusion
  34.0 5.4 copy.15
  39.3 0.0 reduce-scatter.4.cloned.1.call-update
  39.4 0.0 all-reduce.3.cloned.1.call-start
  39.4 58.3 %reduce-scatter.4.cloned.1.call-done = f32[64,1024]{1,0:T(8,128)} async-done(((f32[1024,1024]{1,0:T(8,128)}), f32[64,1024]{1,0:T(8,128)}) %reduce-scatter.4.cloned.1.call-update) | async-done | bytes 262160 | tf_op jit(solution)/shard_map/reduce_scatter | solution.py:87
  97.7 0.0 all-reduce.3.cloned.1.call-update
  97.7 0.0 all-gather.5.cloned.1.call-start
  97.8 102.1 %all-reduce.3.cloned.1.call-done = f32[64,1024]{1,0:T(8,128)} async-done(((f32[64,1024]{1,0:T(8,128)}), f32[64,1024]{1,0:T(8,128)}) %all-reduce.3.cloned.1.call-update) | async-done | bytes 262160 | tf_op jit(solution)/shard_map/psum | solution.py:95
  199.9 1.6 multiply_reduce_fusion
  201.5 21.1 %psum.29 = f32[]{:T(128)} all-reduce(f32[]{:T(128)} %multiply_reduce_fusion), channel_id=1, replica_groups=mesh['rows'=16,'sub'=16] {'sub'}, use_global_device_ids=true, to_apply=%region_3.4 | all-reduce | flops 1 | bytes 8 | tf_op jit(solution)/shard_map/psum | solution.py:96
  223.3 1.7 broadcast_divide_fusion
  224.9 0.0 all-gather.5.cloned.1.call-update
  225.0 0.0 all-gather.7.cloned.1.call-start
  225.0 43.2 %all-gather.5.cloned.1.call-done = f32[1024,1024]{1,0:T(8,128)} async-done(((f32[64,1024]{1,0:T(8,128)}), f32[1024,1024]{1,0:T(8,128)}) %all-gather.5.cloned.1.call-update) | async-done | bytes 4194320 | tf_op jit(solution)/shard_map/all_gather | solution.py:81
  268.2 6.5 %fusion.12 = f32[64,1024]{1,0:T(8,128)S(1)} fusion(f32[64,1024]{1,0:T(8,128)} %broadcast_divide_fusion, f32[1024,1024]{1,0:T(8,128)} %all-gather.5.cloned.1.call-done), kind=kOutput, calls=%fused_computation.26 | convolution fusion | flops 805306368 | bytes 4718592 | tf_op jit(solution)/shard_map/dot_general | solution.py:16
  274.7 0.0 copy-done.2
  274.7 0.0 copy-start.6
  274.8 2.6 fusion.13
  277.4 4.2 fusion.9
  281.6 0.0 copy-done.6
  281.6 3.4 convolution_add_fusion.2
  284.9 0.0 all-gather.7.cloned.1.call-update
  285.0 0.5 all-gather.9.cloned.1.call-start
  285.5 40.1 %all-gather.7.cloned.1.call-done = f32[1024,1024]{1,0:T(8,128)} async-done(((f32[64,1024]{1,0:T(8,128)}), f32[1024,1024]{1,0:T(8,128)}) %all-gather.7.cloned.1.call-update) | async-done | bytes 4194320 | tf_op jit(solution)/shard_map/all_gather | solution.py:81
  325.5 6.5 %fusion.14 = f32[64,1024]{1,0:T(8,128)S(1)} fusion(f32[64,1024]{1,0:T(8,128)} %convolution_add_fusion.2, f32[1024,1024]{1,0:T(8,128)} %all-gather.7.cloned.1.call-done), kind=kOutput, calls=%fused_computation.28 | convolution fusion | flops 805306368 | bytes 4718592 | tf_op jit(solution)/shard_map/dot_general | solution.py:16
  332.0 0.0 copy-done.3
  332.0 0.0 copy-start.5
  332.0 2.6 fusion.15
  334.7 4.2 fusion.8
  338.9 0.0 copy-done.5
  338.9 3.4 convolution_add_fusion.1
  342.2 0.0 all-gather.9.cloned.1.call-update
  342.2 0.2 all-gather.11.cloned.1.call-start
  342.5 40.4 %all-gather.9.cloned.1.call-done = f32[1024,1024]{1,0:T(8,128)} async-done(((f32[64,1024]{1,0:T(8,128)}), f32[1024,1024]{1,0:T(8,128)}) %all-gather.9.cloned.1.call-update) | async-done | bytes 4194320 | tf_op jit(solution)/shard_map/all_gather | solution.py:81
  382.8 6.5 %fusion.16 = f32[64,1024]{1,0:T(8,128)S(1)} fusion(f32[64,1024]{1,0:T(8,128)} %convolution_add_fusion.1, f32[1024,1024]{1,0:T(8,128)} %all-gather.9.cloned.1.call-done), kind=kOutput, calls=%fused_computation.30 | convolution fusion | flops 805306368 | bytes 4718592 | tf_op jit(solution)/shard_map/dot_general | solution.py:16
  389.3 0.0 copy-done.1
  389.3 0.0 copy-start.4
  389.3 2.7 fusion.17
  392.0 0.0 copy-start.8
  392.0 4.2 fusion.7
  396.2 0.0 copy-done.4
  396.2 3.4 fusion.11
  399.6 0.0 all-gather.11.cloned.1.call-update
  399.6 0.0 copy-done.8
  399.6 0.7 all_to_all.27
  400.3 6.0 %all-to-all-start.1 = ((s32[16,4,256]{2,1,0:T(4,128)}), s32[16,4,256]{2,1,0:T(4,128)S(1)}, u32[]{:S(2)}, u32[]{:S(2)}) async-start(s32[16,4,256]{2,1,0:T(4,128)} %all_to_all.27), calls=%async_computation.1 | async-start | bytes 131072 | tf_op jit(solution)/shard_map/all_to_all | solution.py:109
  406.3 31.3 %all-gather.11.cloned.1.call-done = bf16[1024,1024]{1,0:T(8,128)(2,1)} async-done(((bf16[64,1024]{1,0:T(8,128)(2,1)}), bf16[1024,1024]{1,0:T(8,128)(2,1)}) %all-gather.11.cloned.1.call-update) | async-done | bytes 2097168 | tf_op jit(solution)/shard_map/all_gather | solution.py:104
  437.6 3.2 convolution_convert_fusion
  440.8 0.0 all-to-all-done.1
  440.8 6.4 %all-to-all-start = ((bf16[256,16,64]{0,2,1:T(8,128)(2,1)}), bf16[256,16,64]{0,2,1:T(8,128)(2,1)S(1)}, u32[]{:S(2)}, u32[]{:S(2)}) async-start(bf16[256,16,64]{0,2,1:T(8,128)(2,1)} %bitcast.5), calls=%async_computation | async-start | bytes 1048576 | tf_op jit(solution)/shard_map/all_to_all | solution.py:108
  447.1 6.9 %fusion.3 = bf16[4,256]{1,0:T(4,128)(2,1)S(1)} fusion(s32[4,4096]{1,0:T(4,128)S(1)} %bitcast.55), kind=kLoop, calls=%fused_computation.5 | loop fusion | flops 12581888 | bytes 67584 | tf_op jit(solution)/shard_map/while/body/eval_jaxpr/reduce_sum | solution.py:58
  454.1 2.0 copy.14
  456.1 5.9 %all-to-all-done = bf16[256,16,64]{0,2,1:T(8,128)(2,1)S(1)} async-done(((bf16[256,16,64]{0,2,1:T(8,128)(2,1)}), bf16[256,16,64]{0,2,1:T(8,128)(2,1)S(1)}, u32[]{:S(2)}, u32[]{:S(2)}) %all-to-all-start) | async-done | bytes 524320 | tf_op jit(solution)/shard_map/all_to_all | solution.py:108
  462.0 0.3 copy.13
  462.3 0.2 squeeze.11
  462.5 3.2 fusion.10
  465.8 74.2 %all-reduce = (bf16[256,64]{0,1:T(8,128)(2,1)S(1)}, bf16[256,4]{0,1:T(4,128)(2,1)S(1)}) all-reduce(bf16[256,64]{0,1:T(8,128)(2,1)S(1)} %bitcast.57, bf16[256,4]{0,1:T(4,128)(2,1)S(1)} %bitcast.58), channel_id=1, replica_groups=mesh['rows'=16,'sub'=16] {'rows'}, use_global_device_ids=true, to_apply=%region_4.5 | all-reduce | flops 17408 | bytes 69632 | tf_op jit(solution)/shard_map/psum | solution.py:112
  540.0 0.0 copy-done.7
  540.0 0.6 bitcast_divide_fusion
  (5 shorter events, 0.0 us)
Async XLA Ops:
  7.2 24.1 %copy-start = (bf16[256,1024]{1,0:T(8,128)(2,1)S(1)}, bf16[256,1024]{1,0:T(8,128)(2,1)}, u32[]{:S(2)}) copy-start(bf16[256,1024]{1,0:T(8,128)(2,1)} %param.3) | copy-start | bytes 1572868
  7.2 90.5 %reduce-scatter.4.cloned.1.call-start = ((), (), s32[]{:S(2)}) async-start(), calls=%async_computation.8 | async-start | bytes 4456448 | tf_op jit(solution)/shard_map/reduce_scatter | solution.py:87
  39.4 160.5 %all-reduce.3.cloned.1.call-start = ((), (), s32[]{:S(2)}) async-start(), calls=%async_computation.3 | async-start | bytes 524288 | tf_op jit(solution)/shard_map/psum | solution.py:95
  97.7 170.5 %all-gather.5.cloned.1.call-start = ((), (), s32[]{:S(2)}) async-start(), calls=%async_computation.4 | async-start | bytes 4456448 | tf_op jit(solution)/shard_map/all_gather | solution.py:81
  225.0 100.6 %all-gather.7.cloned.1.call-start = ((), (), s32[]{:S(2)}) async-start(), calls=%async_computation.5 | async-start | bytes 4456448 | tf_op jit(solution)/shard_map/all_gather | solution.py:81
  268.2 6.5 %copy-start.2 = (f32[1024,1024]{1,0:T(8,128)S(1)}, f32[1024,1024]{1,0:T(8,128)}, u32[]{:S(2)}) copy-start(f32[1024,1024]{1,0:T(8,128)} %all-gather.5.cloned.1.call-done) | copy-start | bytes 12582916
  274.7 6.8 %copy-start.6 = (f32[64,1024]{1,0:T(8,128)S(1)}, f32[64,1024]{1,0:T(8,128)}, u32[]{:S(2)}) copy-start(f32[64,1024]{1,0:T(8,128)} %broadcast_divide_fusion) | copy-start | bytes 786436
  285.0 97.9 %all-gather.9.cloned.1.call-start = ((), (), s32[]{:S(2)}) async-start(), calls=%async_computation.6 | async-start | bytes 4456448 | tf_op jit(solution)/shard_map/all_gather | solution.py:81
  325.5 6.5 %copy-start.3 = (f32[1024,1024]{1,0:T(8,128)S(1)}, f32[1024,1024]{1,0:T(8,128)}, u32[]{:S(2)}) copy-start(f32[1024,1024]{1,0:T(8,128)} %all-gather.7.cloned.1.call-done) | copy-start | bytes 12582916
  332.0 6.8 %copy-start.5 = (f32[64,1024]{1,0:T(8,128)S(1)}, f32[64,1024]{1,0:T(8,128)}, u32[]{:S(2)}) copy-start(f32[64,1024]{1,0:T(8,128)} %convolution_add_fusion.2) | copy-start | bytes 786436
  342.2 95.4 %all-gather.11.cloned.1.call-start = ((), (), s32[]{:S(2)}) async-start(), calls=%async_computation.7 | async-start | bytes 2228224 | tf_op jit(solution)/shard_map/all_gather | solution.py:104
  382.8 6.5 %copy-start.1 = (f32[1024,1024]{1,0:T(8,128)S(1)}, f32[1024,1024]{1,0:T(8,128)}, u32[]{:S(2)}) copy-start(f32[1024,1024]{1,0:T(8,128)} %all-gather.9.cloned.1.call-done) | copy-start | bytes 12582916
  389.3 6.9 %copy-start.4 = (f32[64,1024]{1,0:T(8,128)S(1)}, f32[64,1024]{1,0:T(8,128)}, u32[]{:S(2)}) copy-start(f32[64,1024]{1,0:T(8,128)} %convolution_add_fusion.1) | copy-start | bytes 786436
  392.0 7.6 %copy-start.8 = (s32[64,256]{1,0:T(8,128)S(1)}, s32[64,256]{1,0:T(8,128)}, u32[]{:S(2)}) copy-start(s32[64,256]{1,0:T(8,128)} %param.4) | copy-start | bytes 196612
  400.3 40.5 %all-to-all-start.1 = ((s32[16,4,256]{2,1,0:T(4,128)}), s32[16,4,256]{2,1,0:T(4,128)S(1)}, u32[]{:S(2)}, u32[]{:S(2)}) async-start(s32[16,4,256]{2,1,0:T(4,128)} %all_to_all.27), calls=%async_computation.1 | async-start | bytes 131072 | tf_op jit(solution)/shard_map/all_to_all | solution.py:109
  440.8 21.2 %all-to-all-start = ((bf16[256,16,64]{0,2,1:T(8,128)(2,1)}), bf16[256,16,64]{0,2,1:T(8,128)(2,1)S(1)}, u32[]{:S(2)}, u32[]{:S(2)}) async-start(bf16[256,16,64]{0,2,1:T(8,128)(2,1)} %bitcast.5), calls=%async_computation | async-start | bytes 1048576 | tf_op jit(solution)/shard_map/all_to_all | solution.py:108
  456.1 83.9 %copy-start.7 = (bf16[256,64]{0,1:T(8,128)(2,1)S(1)}, bf16[256,64]{0,1:T(8,128)(2,1)}, u32[]{:S(2)}) copy-start(bf16[256,64]{0,1:T(8,128)(2,1)} %param.5) | copy-start | bytes 98308
Sparse Core Ops, SparseCore 0:
  39.5 58.1 reduce-scatter.3
  100.9 98.9 all-reduce.2
  225.1 43.1 all-gather.4
  285.1 40.4 all-gather.6
  342.4 40.4 all-gather.8
  399.7 37.8 all-gather.10
where the time goes:
time: 557 us; the launch traced here: 548 us
  waiting for transfers between devices  321 us (58%)
  blocking collectives  114 us (20%)
  matrix products  64.3 us (12%)
  between operations  15.2 us (3%)
  starting transfers between devices  13.3 us (2%)
  other arithmetic  10.9 us (2%)
  local copies, waits for them, and re-layouts  8.64 us (2%)
    all_gather x3, waiting for transfers between devices, collect(): return lax.all_gather(panel, 'sub', axis=0, tiled=True)  124 us
    psum x1, waiting for transfers between devices, body(): cross_panel = lax.psum(partial_panel, 'rows')  102 us
    psum x1, blocking collectives, body(): lax.psum(code_sums.astype(jnp.bfloat16), 'rows').astype(jnp.float32)  74.2 us
    reduce_scatter x1, waiting for transfers between devices, body(): lax.psum_scatter(lax.dot_general(embeddings, decoded, (((0,), (0,)), ((),...  58.3 us
    dot_general x6, matrix products, rows_dot(): lax.dot_general(left, right, (((1,), (1,)), ((), ())), precision=highest,...  31.9 us
    all_gather x1, waiting for transfers between devices, body(): lax.all_gather(panel.astype(jnp.bfloat16), 'sub', axis=0, tiled=True)  31.3 us
    psum x1, blocking collectives, body(): squares = lax.psum(jnp.sum(cross_panel * cross_panel), 'sub')  21.1 us
    all_gather x1, blocking collectives, body(): table = lax.all_gather(codebook, 'sub', axis=1, tiled=True)  18.8 us
  transfers between devices with their start and end apart: 8, of which 7 were waited for; matrix products, arithmetic and copies ran while one was open for 2% of the time, Pallas kernels for 0%

commit v1 on v0

--- a/solution.py
+++ b/solution.py
@@ -10,6 +10,18 @@
 coef_c = 2.0315
 frob_eps = 1e-07
 highest = lax.Precision.HIGHEST
+
+
+def _number_ticks(field_in, mesh_ax):
+    workers = jax.lax.psum(1, mesh_ax)
+    frame_out, clean = (field_in, 0)
+    while 1 << clean < workers:
+        piece_now = jax.lax.ppermute(
+            frame_out, mesh_ax, tuple(((j, j ^ 1 << clean) for j in range(workers)))
+        )
+        frame_out = frame_out + piece_now
+        clean = clean + 1
+    return frame_out
 
 
 def rows_dot(left, right):
@@ -92,7 +104,7 @@
         scatter_dimension=0,
         tiled=True,
     )
-    cross_panel = lax.psum(partial_panel, "rows")
+    cross_panel = _number_ticks(partial_panel, "rows")
     squares = lax.psum(jnp.sum(cross_panel * cross_panel), "sub")
     frob_scale = jnp.sqrt(squares) + frob_eps
     panel = cross_panel / frob_scale

time: 557 us -> 487 us (0.87)
  waiting for transfers between devices: 321 us -> 248 us
  starting transfers between devices: 13.3 us -> 22.9 us
    psum x1 -> x0, waiting for transfers between devices: 102 us -> none  [body(): cross_panel = lax.psum(partial_panel, 'rows')]
    ppermute x0 -> x4, waiting for transfers between devices: none -> 26.5 us  [_number_ticks(): jax.lax.ppermute(frame_out, mesh_ax, tuple(((j, j ^ 1 << clean) for j in...]
    ppermute x0 -> x4, starting transfers between devices: none -> 9.39 us  [_number_ticks(): jax.lax.ppermute(frame_out, mesh_ax, tuple(((j, j ^ 1 << clean) for j in...]
  transfers between devices with their start and end apart: 8 -> 11, of which waited for: 7 -> 10; matrix products, arithmetic and copies ran while one was open for 2% -> 3% of each run, Pallas kernels for 0% -> 0%
where the time goes in v1:
time: 487 us; the launch traced here: 482 us
  waiting for transfers between devices  248 us (51%)
  blocking collectives  114 us (23%)
  matrix products  64.3 us (13%)
  starting transfers between devices  22.9 us (5%)
  between operations  14.9 us (3%)
  other arithmetic  10 us (2%)
  local copies, waits for them, and re-layouts  8.64 us (2%)
    all_gather x3, waiting for transfers between devices, collect(): return lax.all_gather(panel, 'sub', axis=0, tiled=True)  126 us
    psum x1, blocking collectives, body(): lax.psum(code_sums.astype(jnp.bfloat16), 'rows').astype(jnp.float32)  74.2 us
    reduce_scatter x1, waiting for transfers between devices, body(): lax.psum_scatter(lax.dot_general(embeddings, decoded, (((0,), (0,)), ((),...  58.1 us
    dot_general x6, matrix products, rows_dot(): lax.dot_general(left, right, (((1,), (1,)), ((), ())), precision=highest,...  31.9 us
    all_gather x1, waiting for transfers between devices, body(): lax.all_gather(panel.astype(jnp.bfloat16), 'sub', axis=0, tiled=True)  31.3 us
    ppermute x4, waiting for transfers between devices, _number_ticks(): jax.lax.ppermute(frame_out, mesh_ax, tuple(((j, j ^ 1 << clean) for j in...  26.5 us
    psum x1, blocking collectives, body(): squares = lax.psum(jnp.sum(cross_panel * cross_panel), 'sub')  20.7 us
    all_gather x1, blocking collectives, body(): table = lax.all_gather(codebook, 'sub', axis=1, tiled=True)  18.8 us
  transfers between devices with their start and end apart: 11, of which 10 were waited for; matrix products, arithmetic and copies ran while one was open for 3% of the time, Pallas kernels for 0%

profile of v1, /device:TPU:64, one launch (start us, length us, event | category | flops | bytes accessed | tf_op | source)
XLA Modules:
  0.0 482.5 jit_solution(1768068852819949441)
XLA Ops:
  7.2 0.0 copy-start
  7.2 0.0 reduce-scatter.4.cloned.1.call-start
  7.2 18.8 %all_gather.15 = bf16[256,1024]{0,1:T(8,128)(2,1)S(1)} all-gather(bf16[256,64]{0,1:T(8,128)(2,1)} %param.5), channel_id=1, replica_groups=mesh['rows'=16,'sub'=16] {'sub'}, dimensions={1}, use_global_device_ids=true | all-gather | bytes 557056 | tf_op jit(solution)/shard_map/all_gather | solution.py:97
  26.0 5.3 %fusion.6 = bf16[64,256,16]{1,2,0:T(8,128)(2,1)S(1)} fusion(bf16[256,64,16]{0,2,1:T(8,128)(2,1)S(1)} %bitcast.53, s32[64,256]{1,0:T(8,128)} %param.4), kind=kOutput, calls=%fused_computation.9 | convolution fusion | flops 138674176 | bytes 1114112 | tf_op jit(solution)/shard_map/while/body/eval_jaxpr/mnk,kmj->nmj/dot_general | solution.py:49
  31.3 0.0 copy-done
  31.3 2.7 convolution_bitcast_fusion
  34.0 5.4 %copy.16 = f32[1024,1024]{1,0:T(8,128)} copy(f32[1024,1024]{0,1:T(8,128)} %convolution_bitcast_fusion) | data formatting | bytes 8388608
  39.3 0.0 reduce-scatter.4.cloned.1.call-update
  39.4 0.0 all-gather.5.cloned.1.call-start
  39.4 58.1 %reduce-scatter.4.cloned.1.call-done = f32[64,1024]{1,0:T(8,128)} async-done(((f32[1024,1024]{1,0:T(8,128)}), f32[64,1024]{1,0:T(8,128)}) %reduce-scatter.4.cloned.1.call-update) | async-done | bytes 262160 | tf_op jit(solution)/shard_map/reduce_scatter | solution.py:99
  97.6 1.5 collective-permute-start
  99.0 5.6 %collective-permute-done = f32[64,1024]{1,0:T(8,128)S(1)} collective-permute-done((f32[64,1024]{1,0:T(8,128)}, f32[64,1024]{1,0:T(8,128)S(1)}, u32[]{:S(2)}, u32[]{:S(2)}) %collective-permute-start) | collective-permute-done | bytes 262176 | tf_op jit(solution)/shard_map/ppermute | solution.py:19
  104.7 1.0 add.62
  105.6 3.1 collective-permute-start.1
  108.8 6.5 %collective-permute-done.1 = f32[64,1024]{1,0:T(8,128)S(1)} collective-permute-done((f32[64,1024]{1,0:T(8,128)S(1)}, f32[64,1024]{1,0:T(8,128)S(1)}, u32[]{:S(2)}, u32[]{:S(2)}) %collective-permute-start.1) | collective-permute-done | bytes 262176 | tf_op jit(solution)/shard_map/ppermute | solution.py:19
  115.3 1.7 collective-permute-start.2
  117.0 7.6 %collective-permute-done.2 = f32[64,1024]{1,0:T(8,128)S(1)} collective-permute-done((f32[64,1024]{1,0:T(8,128)S(1)}, f32[64,1024]{1,0:T(8,128)S(1)}, u32[]{:S(2)}, u32[]{:S(2)}) %collective-permute-start.2) | collective-permute-done | bytes 262176 | tf_op jit(solution)/shard_map/ppermute | solution.py:19
  124.6 3.1 collective-permute-start.3
  127.7 6.8 %collective-permute-done.3 = f32[64,1024]{1,0:T(8,128)S(1)} collective-permute-done((f32[64,1024]{1,0:T(8,128)S(1)}, f32[64,1024]{1,0:T(8,128)S(1)}, u32[]{:S(2)}, u32[]{:S(2)}) %collective-permute-start.3) | collective-permute-done | bytes 262176 | tf_op jit(solution)/shard_map/ppermute | solution.py:19
  134.5 0.7 multiply_reduce_fusion
  135.2 20.7 %psum.21 = f32[]{:T(128)} all-reduce(f32[]{:T(128)} %get-tuple-element.38), channel_id=1, replica_groups=mesh['rows'=16,'sub'=16] {'sub'}, use_global_device_ids=true, to_apply=%region_2.3 | all-reduce | flops 1 | bytes 8 | tf_op jit(solution)/shard_map/psum | solution.py:108
  156.6 0.7 broadcast_divide_fusion
  157.3 0.0 all-gather.5.cloned.1.call-update
  157.4 0.6 all-gather.7.cloned.1.call-start
  157.9 45.3 %all-gather.5.cloned.1.call-done = f32[1024,1024]{1,0:T(8,128)} async-done(((f32[64,1024]{1,0:T(8,128)}), f32[1024,1024]{1,0:T(8,128)}) %all-gather.5.cloned.1.call-update) | async-done | bytes 4194320 | tf_op jit(solution)/shard_map/all_gather | solution.py:93
  203.2 6.5 %fusion.18 = f32[64,1024]{1,0:T(8,128)S(1)} fusion(f32[64,1024]{1,0:T(8,128)} %broadcast_divide_fusion, f32[1024,1024]{1,0:T(8,128)} %all-gather.5.cloned.1.call-done), kind=kOutput, calls=%fused_computation.30 | convolution fusion | flops 805306368 | bytes 4718592 | tf_op jit(solution)/shard_map/dot_general | solution.py:28
  209.7 0.0 copy-start.6
  209.7 2.6 fusion.19
  212.4 4.2 convolution_multiply_fusion.2
  216.6 3.4 multiply_add_fusion.1
  219.9 0.0 all-gather.7.cloned.1.call-update
  219.9 0.2 all-gather.9.cloned.1.call-start
  220.2 40.4 %all-gather.7.cloned.1.call-done = f32[1024,1024]{1,0:T(8,128)} async-done(((f32[64,1024]{1,0:T(8,128)}), f32[1024,1024]{1,0:T(8,128)}) %all-gather.7.cloned.1.call-update) | async-done | bytes 4194320 | tf_op jit(solution)/shard_map/all_gather | solution.py:93
  260.5 6.5 %fusion.20 = f32[64,1024]{1,0:T(8,128)S(1)} fusion(f32[64,1024]{1,0:T(8,128)} %multiply_add_fusion.1, f32[1024,1024]{1,0:T(8,128)} %all-gather.7.cloned.1.call-done), kind=kOutput, calls=%fused_computation.32 | convolution fusion | flops 805306368 | bytes 4718592 | tf_op jit(solution)/shard_map/dot_general | solution.py:28
  267.0 0.0 copy-start.5
  267.0 2.6 fusion.21
  269.7 4.2 fusion.8
  273.9 3.4 multiply_add_fusion
  277.2 0.0 all-gather.9.cloned.1.call-update
  277.2 0.3 all-gather.11.cloned.1.call-start
  277.5 40.3 %all-gather.9.cloned.1.call-done = f32[1024,1024]{1,0:T(8,128)} async-done(((f32[64,1024]{1,0:T(8,128)}), f32[1024,1024]{1,0:T(8,128)}) %all-gather.9.cloned.1.call-update) | async-done | bytes 4194320 | tf_op jit(solution)/shard_map/all_gather | solution.py:93
  317.8 6.5 %fusion.22 = f32[64,1024]{1,0:T(8,128)S(1)} fusion(f32[64,1024]{1,0:T(8,128)} %multiply_add_fusion, f32[1024,1024]{1,0:T(8,128)} %all-gather.9.cloned.1.call-done), kind=kOutput, calls=%fused_computation.34 | convolution fusion | flops 805306368 | bytes 4718592 | tf_op jit(solution)/shard_map/dot_general | solution.py:28
  324.3 0.0 copy-start.4
  324.3 2.7 fusion.23
  327.0 0.0 copy-start.8
  327.0 4.2 fusion.7
  331.2 0.0 copy-done.4
  331.2 3.4 fusion.17
  334.6 0.0 all-gather.11.cloned.1.call-update
  334.6 0.0 copy-done.8
  334.6 0.7 all_to_all.27
  335.3 6.0 %all-to-all-start.1 = ((s32[16,4,256]{2,1,0:T(4,128)}), s32[16,4,256]{2,1,0:T(4,128)S(1)}, u32[]{:S(2)}, u32[]{:S(2)}) async-start(s32[16,4,256]{2,1,0:T(4,128)} %all_to_all.27), calls=%async_computation.1 | async-start | bytes 131072 | tf_op jit(solution)/shard_map/all_to_all | solution.py:121
  341.3 31.3 %all-gather.11.cloned.1.call-done = bf16[1024,1024]{1,0:T(8,128)(2,1)} async-done(((bf16[64,1024]{1,0:T(8,128)(2,1)}), bf16[1024,1024]{1,0:T(8,128)(2,1)}) %all-gather.11.cloned.1.call-update) | async-done | bytes 2097168 | tf_op jit(solution)/shard_map/all_gather | solution.py:116
  372.6 3.2 convolution_convert_fusion
  375.7 0.0 all-to-all-done.1
  375.7 6.4 %all-to-all-start = ((bf16[256,16,64]{0,2,1:T(8,128)(2,1)}), bf16[256,16,64]{0,2,1:T(8,128)(2,1)S(1)}, u32[]{:S(2)}, u32[]{:S(2)}) async-start(bf16[256,16,64]{0,2,1:T(8,128)(2,1)} %bitcast.5), calls=%async_computation | async-start | bytes 1048576 | tf_op jit(solution)/shard_map/all_to_all | solution.py:120
  382.2 6.9 %fusion.3 = bf16[4,256]{1,0:T(4,128)(2,1)S(1)} fusion(s32[4,4096]{1,0:T(4,128)S(1)} %bitcast.54), kind=kLoop, calls=%fused_computation.5 | loop fusion | flops 12581888 | bytes 67584 | tf_op jit(solution)/shard_map/while/body/eval_jaxpr/reduce_sum | solution.py:70
  389.1 2.0 copy.15
  391.1 5.9 %all-to-all-done = bf16[256,16,64]{0,2,1:T(8,128)(2,1)S(1)} async-done(((bf16[256,16,64]{0,2,1:T(8,128)(2,1)}), bf16[256,16,64]{0,2,1:T(8,128)(2,1)S(1)}, u32[]{:S(2)}, u32[]{:S(2)}) %all-to-all-start) | async-done | bytes 524320 | tf_op jit(solution)/shard_map/all_to_all | solution.py:120
  397.0 0.3 copy.14
  397.3 0.2 squeeze.11
  397.6 3.2 fusion.9
  400.8 74.2 %all-reduce = (bf16[256,64]{0,1:T(8,128)(2,1)S(1)}, bf16[256,4]{0,1:T(4,128)(2,1)S(1)}) all-reduce(bf16[256,64]{0,1:T(8,128)(2,1)S(1)} %bitcast.56, bf16[256,4]{0,1:T(4,128)(2,1)S(1)} %bitcast.57), channel_id=1, replica_groups=mesh['rows'=16,'sub'=16] {'rows'}, use_global_device_ids=true, to_apply=%region_3.4 | all-reduce | flops 17408 | bytes 69632 | tf_op jit(solution)/shard_map/psum | solution.py:124
  475.0 0.6 bitcast_divide_fusion
  (13 shorter events, 0.1 us)
Async XLA Ops:
  7.2 24.1 %copy-start = (bf16[256,1024]{1,0:T(8,128)(2,1)S(1)}, bf16[256,1024]{1,0:T(8,128)(2,1)}, u32[]{:S(2)}) copy-start(bf16[256,1024]{1,0:T(8,128)(2,1)} %param.3) | copy-start | bytes 1572868
  7.2 90.4 %reduce-scatter.4.cloned.1.call-start = ((), (), s32[]{:S(2)}) async-start(), calls=%async_computation.7 | async-start | bytes 4456448 | tf_op jit(solution)/shard_map/reduce_scatter | solution.py:99
  39.4 163.9 %all-gather.5.cloned.1.call-start = ((), (), s32[]{:S(2)}) async-start(), calls=%async_computation.3 | async-start | bytes 4456448 | tf_op jit(solution)/shard_map/all_gather | solution.py:93
  97.6 7.1 %collective-permute-start = (f32[64,1024]{1,0:T(8,128)}, f32[64,1024]{1,0:T(8,128)S(1)}, u32[]{:S(2)}, u32[]{:S(2)}) collective-permute-start(f32[64,1024]{1,0:T(8,128)} %reduce-scatter.4.cloned.1.call-done), channel_id=1, source_target_pairs={{0,16},{16,0},{32,48},{48,32},{64,80},{80,64},{96,112},{112,96},{1... | collective-permute-start | bytes 786440 | tf_op jit(solution)/shard_map/ppermute | solution.py:19
  105.6 9.6 %collective-permute-start.1 = (f32[64,1024]{1,0:T(8,128)S(1)}, f32[64,1024]{1,0:T(8,128)S(1)}, u32[]{:S(2)}, u32[]{:S(2)}) collective-permute-start(f32[64,1024]{1,0:T(8,128)S(1)} %add.62), channel_id=1, source_target_pairs={{0,32},{16,48},{32,0},{48,16},{64,96},{80,112},{96,64},{112,80},{1... | collective-permute-start | bytes 786440 | tf_op jit(solution)/shard_map/ppermute | solution.py:19
  115.3 9.3 %collective-permute-start.2 = (f32[64,1024]{1,0:T(8,128)S(1)}, f32[64,1024]{1,0:T(8,128)S(1)}, u32[]{:S(2)}, u32[]{:S(2)}) collective-permute-start(f32[64,1024]{1,0:T(8,128)S(1)} %add.63), channel_id=1, source_target_pairs={{0,64},{16,80},{32,96},{48,112},{64,0},{80,16},{96,32},{112,48},{1... | collective-permute-start | bytes 786440 | tf_op jit(solution)/shard_map/ppermute | solution.py:19
  124.6 9.9 %collective-permute-start.3 = (f32[64,1024]{1,0:T(8,128)S(1)}, f32[64,1024]{1,0:T(8,128)S(1)}, u32[]{:S(2)}, u32[]{:S(2)}) collective-permute-start(f32[64,1024]{1,0:T(8,128)S(1)} %add.64), channel_id=1, source_target_pairs={{0,128},{16,144},{32,160},{48,176},{64,192},{80,208},{96,224},{112... | collective-permute-start | bytes 786440 | tf_op jit(solution)/shard_map/ppermute | solution.py:19
  157.4 103.2 %all-gather.7.cloned.1.call-start = ((), (), s32[]{:S(2)}) async-start(), calls=%async_computation.4 | async-start | bytes 4456448 | tf_op jit(solution)/shard_map/all_gather | solution.py:93
  203.2 6.5 %copy-start.1 = (f32[1024,1024]{1,0:T(8,128)S(1)}, f32[1024,1024]{1,0:T(8,128)}, u32[]{:S(2)}) copy-start(f32[1024,1024]{1,0:T(8,128)} %all-gather.5.cloned.1.call-done) | copy-start | bytes 12582916
  209.7 6.8 %copy-start.6 = (f32[64,1024]{1,0:T(8,128)S(1)}, f32[64,1024]{1,0:T(8,128)}, u32[]{:S(2)}) copy-start(f32[64,1024]{1,0:T(8,128)} %broadcast_divide_fusion) | copy-start | bytes 786436
  219.9 97.9 %all-gather.9.cloned.1.call-start = ((), (), s32[]{:S(2)}) async-start(), calls=%async_computation.5 | async-start | bytes 4456448 | tf_op jit(solution)/shard_map/all_gather | solution.py:93
  260.5 6.5 %copy-start.3 = (f32[1024,1024]{1,0:T(8,128)S(1)}, f32[1024,1024]{1,0:T(8,128)}, u32[]{:S(2)}) copy-start(f32[1024,1024]{1,0:T(8,128)} %all-gather.7.cloned.1.call-done) | copy-start | bytes 12582916
  267.0 6.8 %copy-start.5 = (f32[64,1024]{1,0:T(8,128)S(1)}, f32[64,1024]{1,0:T(8,128)}, u32[]{:S(2)}) copy-start(f32[64,1024]{1,0:T(8,128)} %multiply_add_fusion.1) | copy-start | bytes 786436
  277.2 95.4 %all-gather.11.cloned.1.call-start = ((), (), s32[]{:S(2)}) async-start(), calls=%async_computation.6 | async-start | bytes 2228224 | tf_op jit(solution)/shard_map/all_gather | solution.py:116
  317.8 6.5 %copy-start.2 = (f32[1024,1024]{1,0:T(8,128)S(1)}, f32[1024,1024]{1,0:T(8,128)}, u32[]{:S(2)}) copy-start(f32[1024,1024]{1,0:T(8,128)} %all-gather.9.cloned.1.call-done) | copy-start | bytes 12582916
  324.3 6.9 %copy-start.4 = (f32[64,1024]{1,0:T(8,128)S(1)}, f32[64,1024]{1,0:T(8,128)}, u32[]{:S(2)}) copy-start(f32[64,1024]{1,0:T(8,128)} %multiply_add_fusion) | copy-start | bytes 786436
  327.0 7.6 %copy-start.8 = (s32[64,256]{1,0:T(8,128)S(1)}, s32[64,256]{1,0:T(8,128)}, u32[]{:S(2)}) copy-start(s32[64,256]{1,0:T(8,128)} %param.4) | copy-start | bytes 196612
  335.3 40.5 %all-to-all-start.1 = ((s32[16,4,256]{2,1,0:T(4,128)}), s32[16,4,256]{2,1,0:T(4,128)S(1)}, u32[]{:S(2)}, u32[]{:S(2)}) async-start(s32[16,4,256]{2,1,0:T(4,128)} %all_to_all.27), calls=%async_computation.1 | async-start | bytes 131072 | tf_op jit(solution)/shard_map/all_to_all | solution.py:121
  375.7 21.3 %all-to-all-start = ((bf16[256,16,64]{0,2,1:T(8,128)(2,1)}), bf16[256,16,64]{0,2,1:T(8,128)(2,1)S(1)}, u32[]{:S(2)}, u32[]{:S(2)}) async-start(bf16[256,16,64]{0,2,1:T(8,128)(2,1)} %bitcast.5), calls=%async_computation | async-start | bytes 1048576 | tf_op jit(solution)/shard_map/all_to_all | solution.py:120
  391.1 83.9 %copy-start.7 = (bf16[256,64]{0,1:T(8,128)(2,1)S(1)}, bf16[256,64]{0,1:T(8,128)(2,1)}, u32[]{:S(2)}) copy-start(bf16[256,64]{0,1:T(8,128)(2,1)} %param.5) | copy-start | bytes 98308
Sparse Core Ops, SparseCore 0:
  39.5 58.0 reduce-scatter.3
  157.5 45.7 all-gather.4
  220.1 40.4 all-gather.6
  277.4 40.4 all-gather.8
  334.7 37.8 all-gather.10
